TPU v7x, 256 devices: a whole 4x4x8 slice. The times are simulated.
256 devices in a mesh: cent: 8 (over z), dp: 32 (over x, y, core).
Axes of the slice: x: 4, y: 4, z: 8, core: 2. Of those that a mesh axis runs over, the one named last changes fastest.
Arguments:
- points: bfloat16 [32768, 1024], P('dp'), may hold values from -6 to 6
- cluster_ids: int32 [32768, 1], P('dp'), may hold values from 0 to 63; in each aligned block of 1024 rows (0 to 1023, 1024 to 2047, ...) at most 64 rows name the same one
- centroids: bfloat16 [8192, 1024], P('cent'), may hold values from -6 to 6
- sub_centroids: bfloat16 [64, 1024, 1024], P('dp', 'cent'), may hold values from -6 to 6
Outputs:
- assign: bfloat16 [32768, 8192], P('dp', 'cent')
- sub_assign: bfloat16 [32768, 1024], P('dp', 'cent')
Inputs may be any that keep to these rules, and one draw needn't show every extreme that they name: `cluster_ids`: among the 1024 points of one index of dp, no level-two cluster holds more than 64 points; some cluster holds exactly 64 in some block.
All inputs are finite; a program needn't handle non-finite values.
Results may differ from a plain program's by a relative error of at most 0.001.
Values may be sent and summed in bfloat16 or wider, within the bound.
No kernel may reach another device: no remote copies, remote signals or barrier semaphores. Data moves between devices by JAX's collectives and lax.ppermute only.
A program may use at most 128 MiB of HBM per device.

v0:
```python
import jax
import jax.numpy as jnp
from jax import lax
from jax.sharding import PartitionSpec as P

CAP = 64
ITERS = 3
EPS = 1e-06
TAU = 0.05


def inverse_norm(rows):
    values = rows.astype(jnp.float32)
    return lax.rsqrt(jnp.mean(values * values, axis=-1) + EPS)


def shards(points, cluster_ids, centroids, sub_centroids):
    pts_count = points.shape[0]
    width = points.shape[1]
    dp_count = lax.axis_size("dp")
    cent_count = lax.axis_size("cent")
    group_dev = sub_centroids.shape[0]
    sub_dev = sub_centroids.shape[1]
    clusters = group_dev * dp_count
    total_cent = centroids.shape[0] * cent_count
    total_sub = sub_dev * cent_count
    inv_x = inverse_norm(points)
    inv_c = inverse_norm(centroids)
    inv_u = inverse_norm(sub_centroids)
    scores = jnp.einsum("pd,kd->pk", points, centroids, preferred_element_type=jnp.float32)
    expo = jnp.exp(scores * inv_x[:, None] * inv_c[None, :] * (1.0 / (width * TAU)))
    row_scale = jnp.ones((pts_count,), jnp.float32)
    col_scale = jnp.ones((centroids.shape[0],), jnp.float32)
    row_part = row_scale
    for step in range(ITERS):
        col_part = jnp.dot(row_scale, expo, precision=lax.Precision.HIGHEST)
        col_scale = 1.0 / lax.psum(col_part, "dp")
        row_part = jnp.dot(expo, col_scale, precision=lax.Precision.HIGHEST)
        if step + 1 < ITERS:
            row_scale = 1.0 / lax.psum(row_part, "cent")
    ids = cluster_ids[:, 0]
    labels = lax.broadcasted_iota(jnp.int32, (pts_count, clusters), 1)
    onehot = ids[:, None] == labels
    positions = lax.broadcasted_iota(jnp.int32, (pts_count, pts_count), 0)
    earlier = (positions > positions.T).astype(jnp.bfloat16)
    before = jnp.dot(earlier, onehot.astype(jnp.bfloat16), preferred_element_type=jnp.float32)
    rank = jnp.sum(before * onehot.astype(jnp.float32), axis=1).astype(jnp.int32)
    slot = ids * CAP + rank
    buffer = jnp.zeros((clusters * CAP, width), jnp.bfloat16).at[slot].set(points)
    scale_two = 1.0 / (width * TAU)
    outgoing = buffer.reshape(dp_count, group_dev * CAP, width)
    arrived = lax.all_to_all(outgoing, "dp", split_axis=0, concat_axis=0, tiled=True)
    arrived = arrived.reshape(dp_count, group_dev, CAP, width)
    inv_rows = inverse_norm(arrived)
    dots = jnp.einsum("sgcd,gkd->sgck", arrived, sub_centroids, preferred_element_type=jnp.float32)
    weights = jnp.exp(dots * inv_rows[..., None] * inv_u[None, :, None, :] * scale_two)
    weights = weights.reshape(dp_count, group_dev * CAP, sub_dev)
    returned = lax.all_to_all(weights, "dp", split_axis=0, concat_axis=0, tiled=True)
    slot_weights = returned.reshape(clusters * CAP, sub_dev)
    point_weights = slot_weights[slot]
    denom_part = jnp.sum(point_weights, axis=1)
    row_total = lax.psum(row_part, "cent")
    denominator = lax.psum(denom_part, "cent")
    row_scale = 1.0 / row_total
    assign = (expo * row_scale[:, None] * col_scale[None, :] * total_cent).astype(jnp.bfloat16)
    sub_assign = (total_sub * point_weights / denominator[:, None]).astype(jnp.bfloat16)
    return (assign, sub_assign)


def solution(mesh):
    return jax.shard_map(
        shards,
        mesh=mesh,
        in_specs=(P("dp", None), P("dp", None), P("cent", None), P("dp", "cent", None)),
        out_specs=(P("dp", "cent"), P("dp", "cent")),
        check_vma=False,
    )
```

profile of v0, /device:TPU:0, one launch (start us, length us, event | category | flops | bytes accessed | tf_op | source)
XLA Modules:
  0.0 412.9 jit_solution(17542967821555174308)
XLA Ops:
  0.6 1.4 fusion.11
  2.0 0.7 compare_select_fusion
  2.7 10.8 %scatter_custom_fusion = bf16[4096,1024]{1,0:T(8,128)(2,1)} fusion(s32[1024]{0:T(1024)S(1)} %bitcast.56, bf16[1024,1024]{1,0:T(8,128)(2,1)} %param.4, bf16[]{:T(256)} %constant.6.clone.1), kind=kCustom, calls=%fused_computation.6 | custom fusion | bytes 8389120 | tf_op jit(solution)/shard_map/scatter | solution.py:49
  13.5 0.0 copy-start.1
  13.5 6.1 %all-to-all-start = ((bf16[32,128,1024]{2,1,0:T(8,128)(2,1)}), bf16[32,128,1024]{2,1,0:T(8,128)(2,1)}, u32[]{:S(2)}, u32[]{:S(2)}) async-start(bf16[32,128,1024]{2,1,0:T(8,128)(2,1)} %bitcast.51), calls=%async_computation | async-start | bytes 16777216 | tf_op jit(solution)/shard_map/all_to_all | solution.py:52
  19.6 0.0 copy-start.2
  19.6 2.2 multiply_reduce_fusion.1
  21.8 0.0 copy-done.1
  21.8 0.5 multiply_reduce_fusion.2
  22.3 0.0 copy-done.2
  22.3 2.6 multiply_exponential_fusion
  24.9 0.0 copy-start
  24.9 1.9 copy-done
  26.9 0.0 copy-start.3
  26.9 2.1 fusion.14
  28.9 141.6 %psum.49 = f32[1024]{0:T(1024)S(1)} all-reduce(f32[1024]{0:T(1024)S(1)} %bitcast.55), channel_id=1, replica_groups=mesh['cent'=8,'dp'=32] {'dp'}, use_global_device_ids=true, to_apply=%region_2.0 | all-reduce | flops 1024 | bytes 8192 | tf_op jit(solution)/shard_map/psum | solution.py:37
  170.5 5.8 %fusion.17 = f32[1,1024]{1,0:T(1,128)S(1)} fusion(f32[1024,1024]{1,0:T(8,128)} %copy-done, f32[1024,1]{0,1:T(1,128)S(1)} %bitcast.61), kind=kOutput, calls=%fused_computation.39 | convolution fusion | flops 12582912 | bytes 4202496 | tf_op jit(solution)/shard_map/dot_general | solution.py:38
  176.3 20.0 %psum.50 = f32[1024]{0:T(1024)S(1)} all-reduce(f32[1024]{0:T(1024)S(1)} %bitcast.62), channel_id=1, replica_groups=mesh['cent'=8,'dp'=32] {'cent'}, use_global_device_ids=true, to_apply=%region_3.0 | all-reduce | flops 1024 | bytes 8192 | tf_op jit(solution)/shard_map/psum | solution.py:40
  196.3 0.0 copy-done.3
  196.3 0.2 multiply_reduce_fusion.3
  196.5 0.0 all-to-all-done
  196.5 5.1 %multiply_reduce_fusion = f32[32,128]{1,0:T(8,128)S(1)} fusion(bf16[32,128,1024]{2,1,0:T(8,128)(2,1)} %all-to-all-done), kind=kLoop, calls=%fused_computation.2 | loop fusion | flops 12578816 | bytes 8404992 | tf_op jit(solution)/shard_map/reduce_sum | solution.py:14
  201.6 0.1 rsqrt.34
  201.7 4.8 %fusion.7 = f32[32,2,64,128]{3,2,0,1:T(8,128)S(1)} fusion(bf16[32,2,64,1024]{3,2,1,0:T(8,128)(2,1)} %bitcast.16, f32[2,128]{1,0:T(2,128)S(1)} %add_rsqrt_fusion.3, f32[32,2,64]{2,0,1:T(8,128)S(1)} %copy.7, bf16[2,128,1024]{2,1,0:T(8,128)(2,1)S(1)} %copy-done.3), kind=kOutput, calls=%fused_computation.16 | convolution fusion | flops 1075314688 | bytes 11027456 | tf_op jit(solution)/shard_map/sgcd,gkd->sgck/dot_general | solution.py:55
  206.5 1.5 copy.8
  208.0 5.4 %all-to-all-start.1 = ((f32[32,128,128]{2,1,0:T(8,128)}), f32[32,128,128]{2,1,0:T(8,128)S(1)}, u32[]{:S(2)}, u32[]{:S(2)}) async-start(f32[32,128,128]{2,1,0:T(8,128)} %bitcast.53), calls=%async_computation.1 | async-start | bytes 4194304 | tf_op jit(solution)/shard_map/all_to_all | solution.py:58
  213.4 4.3 %fusion.18 = f32[1,1024]{1,0:T(1,128)S(1)} fusion(f32[1024,1]{0,1:T(1,128)S(1)} %bitcast.59, f32[1024,1024]{1,0:T(8,128)} %copy-done), kind=kOutput, calls=%fused_computation.40 | convolution fusion | flops 12582912 | bytes 4202496 | tf_op jit(solution)/shard_map/dot_general | solution.py:36
  217.6 78.1 %psum.51 = f32[1024]{0:T(1024)S(1)} all-reduce(f32[1024]{0:T(1024)S(1)} %bitcast.63), channel_id=1, replica_groups=mesh['cent'=8,'dp'=32] {'dp'}, use_global_device_ids=true, to_apply=%region_4.0 | all-reduce | flops 1024 | bytes 8192 | tf_op jit(solution)/shard_map/psum | solution.py:37
  295.7 5.8 %fusion.19 = f32[1,1024]{1,0:T(1,128)S(1)} fusion(f32[1024,1024]{1,0:T(8,128)} %copy-done, f32[1024,1]{0,1:T(1,128)S(1)} %bitcast.64), kind=kOutput, calls=%fused_computation.41 | convolution fusion | flops 12582912 | bytes 4202496 | tf_op jit(solution)/shard_map/dot_general | solution.py:38
  301.5 14.2 %psum.52 = f32[1024]{0:T(1024)S(1)} all-reduce(f32[1024]{0:T(1024)S(1)} %bitcast.65), channel_id=1, replica_groups=mesh['cent'=8,'dp'=32] {'cent'}, use_global_device_ids=true, to_apply=%region_5.0 | all-reduce | flops 1024 | bytes 8192 | tf_op jit(solution)/shard_map/psum | solution.py:40
  315.7 4.3 %fusion.20 = f32[1,1024]{1,0:T(1,128)S(1)} fusion(f32[1024,1]{0,1:T(1,128)S(1)} %bitcast.66, f32[1024,1024]{1,0:T(8,128)} %copy-done), kind=kOutput, calls=%fused_computation.42 | convolution fusion | flops 12582912 | bytes 4202496 | tf_op jit(solution)/shard_map/dot_general | solution.py:36
  319.9 62.7 %psum.53 = f32[1024]{0:T(1024)S(1)} all-reduce(f32[1024]{0:T(1024)S(1)} %bitcast.67), channel_id=1, replica_groups=mesh['cent'=8,'dp'=32] {'dp'}, use_global_device_ids=true, to_apply=%region_6.0 | all-reduce | flops 1024 | bytes 8192 | tf_op jit(solution)/shard_map/psum | solution.py:37
  382.6 5.8 %fusion.21 = f32[1,1024]{1,0:T(1,128)S(1)} fusion(f32[1024,1024]{1,0:T(8,128)} %copy-done, f32[1024,1]{0,1:T(1,128)S(1)} %bitcast.54), kind=kOutput, calls=%fused_computation.43 | convolution fusion | flops 12582912 | bytes 4202496 | tf_op jit(solution)/shard_map/dot_general | solution.py:38
  388.4 0.0 all-to-all-done.1
  388.4 2.8 gather_fusion
  391.2 0.2 reduce_sum.59
  391.4 16.5 %all-reduce = (f32[1024]{0:T(1024)S(1)}, f32[1024]{0:T(1024)S(1)}) all-reduce(f32[1024]{0:T(1024)S(1)} %bitcast.60, f32[1024]{0:T(1024)S(1)} %reduce_sum.59), channel_id=1, replica_groups=mesh['cent'=8,'dp'=32] {'cent'}, use_global_device_ids=true, to_apply=%region_7.0 | all-reduce | flops 2048 | bytes 16384 | tf_op jit(solution)/shard_map/psum | solution.py:62
  407.9 4.0 multiply_convert_fusion
  412.0 0.9 divide_convert_fusion
  (13 shorter events, 0.1 us)
Async XLA Ops:
  13.5 8.3 %copy-start.1 = (bf16[1024,1024]{1,0:T(8,128)(2,1)S(1)}, bf16[1024,1024]{1,0:T(8,128)(2,1)}, u32[]{:S(2)}) copy-start(bf16[1024,1024]{1,0:T(8,128)(2,1)} %param.4) | copy-start | bytes 6291460
  13.5 183.0 %all-to-all-start = ((bf16[32,128,1024]{2,1,0:T(8,128)(2,1)}), bf16[32,128,1024]{2,1,0:T(8,128)(2,1)}, u32[]{:S(2)}, u32[]{:S(2)}) async-start(bf16[32,128,1024]{2,1,0:T(8,128)(2,1)} %bitcast.51), calls=%async_computation | async-start | bytes 16777216 | tf_op jit(solution)/shard_map/all_to_all | solution.py:52
  19.6 2.7 copy-start.2
  24.9 1.9 copy-start
  26.9 169.4 %copy-start.3 = (bf16[2,128,1024]{2,1,0:T(8,128)(2,1)S(1)}, bf16[2,128,1024]{2,1,0:T(8,128)(2,1)}, u32[]{:S(2)}) copy-start(bf16[2,128,1024]{2,1,0:T(8,128)(2,1)} %param.7) | copy-start | bytes 1572868
  208.0 180.4 %all-to-all-start.1 = ((f32[32,128,128]{2,1,0:T(8,128)}), f32[32,128,128]{2,1,0:T(8,128)S(1)}, u32[]{:S(2)}, u32[]{:S(2)}) async-start(f32[32,128,128]{2,1,0:T(8,128)} %bitcast.53), calls=%async_computation.1 | async-start | bytes 4194304 | tf_op jit(solution)/shard_map/all_to_all | solution.py:58
where the time goes:
time: 414 us; the launch traced here: 413 us
  blocking collectives  333 us (80%)
  matrix products  36.6 us (9%)
  local copies, waits for them, and re-layouts  17.1 us (4%)
  other arithmetic  13.9 us (3%)
  starting transfers between devices  11.5 us (3%)
    psum x3, blocking collectives, shards(): col_scale = 1.0 / lax.psum(col_part, 'dp')  282 us
    psum x2, blocking collectives, shards(): row_scale = 1.0 / lax.psum(row_part, 'cent')  34.2 us
    dot_general x3, matrix products, shards(): row_part = jnp.dot(expo, col_scale, precision=lax.Precision.HIGHEST)  17.3 us
    psum x1, blocking collectives, shards(): row_total = lax.psum(row_part, 'cent')  16.5 us
    scatter x1, local copies, waits for them, and re-layouts, shards(): jnp.zeros((clusters * CAP, width), jnp.bfloat16).at[slot].set(points)  10.8 us
    dot_general x3, matrix products, shards(): col_part = jnp.dot(row_scale, expo, precision=lax.Precision.HIGHEST)  10.6 us
  transfers between devices with their start and end apart: 2, of which 0 were waited for; matrix products, arithmetic and copies ran while one was open for 8% of the time, Pallas kernels for 0%

commit v1 on v0

--- a/solution.py
+++ b/solution.py
@@ -59,7 +59,10 @@
     slot_weights = returned.reshape(clusters * CAP, sub_dev)
     point_weights = slot_weights[slot]
     denom_part = jnp.sum(point_weights, axis=1)
-    row_total = lax.psum(row_part, "cent")
+    peers, row_total = (lax.axis_size("cent"), row_part)
+    for far in [1 << k for k in range(peers.bit_length() - 1)]:
+        swap = [(i, i ^ far) for i in range(peers)]
+        row_total = row_total + lax.ppermute(row_total, "cent", swap)
     denominator = lax.psum(denom_part, "cent")
     row_scale = 1.0 / row_total
     assign = (expo * row_scale[:, None] * col_scale[None, :] * total_cent).astype(jnp.bfloat16)

time: 414 us -> 455 us (1.099)
  waiting for transfers between devices: 0.01 us -> 115 us
  blocking collectives: 333 us -> 238 us
  starting transfers between devices: 11.5 us -> 30.3 us
    all_to_all x1, waiting for transfers between devices: 0.01 us -> 106 us  [shards(): lax.all_to_all(outgoing, 'dp', split_axis=0, concat_axis=0, tiled=True)]
    psum x3, blocking collectives: 282 us -> 204 us  [shards(): col_scale = 1.0 / lax.psum(col_part, 'dp')]
    psum x1 -> x0, blocking collectives: 16.5 us -> none  [shards(): row_total = lax.psum(row_part, 'cent')]
    all_to_all x1, starting transfers between devices: 5.4 us -> 18.4 us  [shards(): lax.all_to_all(weights, 'dp', split_axis=0, concat_axis=0, tiled=True)]
    ppermute x0 -> x3, waiting for transfers between devices: none -> 9.11 us  [shards(): row_total = row_total + lax.ppermute(row_total, 'cent', swap)]
    ppermute x0 -> x3, starting transfers between devices: none -> 5.65 us  [shards(): row_total = row_total + lax.ppermute(row_total, 'cent', swap)]
  transfers between devices with their start and end apart: 2 -> 5, of which waited for: 0 -> 4; matrix products, arithmetic and copies ran while one was open for 8% -> 6% of each run, Pallas kernels for 0% -> 0%
where the time goes in v1:
time: 455 us; the launch traced here: 452 us
  blocking collectives  238 us (52%)
  waiting for transfers between devices  115 us (25%)
  matrix products  40.8 us (9%)
  starting transfers between devices  30.3 us (7%)
  local copies, waits for them, and re-layouts  15.2 us (3%)
  other arithmetic  11.7 us (3%)
    psum x3, blocking collectives, shards(): col_scale = 1.0 / lax.psum(col_part, 'dp')  204 us
    all_to_all x1, waiting for transfers between devices, shards(): lax.all_to_all(outgoing, 'dp', split_axis=0, concat_axis=0, tiled=True)  106 us
    psum x2, blocking collectives, shards(): row_scale = 1.0 / lax.psum(row_part, 'cent')  34.6 us
    all_to_all x1, starting transfers between devices, shards(): lax.all_to_all(weights, 'dp', split_axis=0, concat_axis=0, tiled=True)  18.4 us
    dot_general x3, matrix products, shards(): row_part = jnp.dot(expo, col_scale, precision=lax.Precision.HIGHEST)  17.4 us
    dot_general x3, matrix products, shards(): col_part = jnp.dot(row_scale, expo, precision=lax.Precision.HIGHEST)  12.8 us
    scatter x1, local copies, waits for them, and re-layouts, shards(): jnp.zeros((clusters * CAP, width), jnp.bfloat16).at[slot].set(points)  10.8 us
    ppermute x3, waiting for transfers between devices, shards(): row_total = row_total + lax.ppermute(row_total, 'cent', swap)  9.11 us
  transfers between devices with their start and end apart: 5, of which 4 were waited for; matrix products, arithmetic and copies ran while one was open for 6% of the time, Pallas kernels for 0%

profile of v1, /device:TPU:0, one launch (start us, length us, event | category | flops | bytes accessed | tf_op | source)
XLA Modules:
  0.0 452.2 jit_solution(3247256039367937655)
XLA Ops:
  0.6 1.4 fusion.11
  2.0 0.7 compare_select_fusion
  2.7 10.8 %scatter_custom_fusion = bf16[4096,1024]{1,0:T(8,128)(2,1)} fusion(s32[1024]{0:T(1024)S(1)} %bitcast.56, bf16[1024,1024]{1,0:T(8,128)(2,1)} %param.4, bf16[]{:T(256)} %constant.6.clone.1), kind=kCustom, calls=%fused_computation.6 | custom fusion | bytes 8389120 | tf_op jit(solution)/shard_map/scatter | solution.py:49
  13.5 0.0 copy-start.3
  13.5 0.0 copy-start.1
  13.5 6.2 %all-to-all-start = ((bf16[32,128,1024]{2,1,0:T(8,128)(2,1)}), bf16[32,128,1024]{2,1,0:T(8,128)(2,1)}, u32[]{:S(2)}, u32[]{:S(2)}) async-start(bf16[32,128,1024]{2,1,0:T(8,128)(2,1)} %bitcast.51), calls=%async_computation | async-start | bytes 16777216 | tf_op jit(solution)/shard_map/all_to_all | solution.py:52
  19.7 0.0 copy-done.3
  19.7 0.0 copy-start.2
  19.7 0.2 multiply_reduce_fusion.3
  19.9 2.2 multiply_reduce_fusion.1
  22.1 0.0 copy-done.1
  22.1 0.5 multiply_reduce_fusion.2
  22.6 0.0 copy-done.2
  22.6 4.5 multiply_exponential_fusion
  27.1 106.1 %all-to-all-done = bf16[32,128,1024]{2,1,0:T(8,128)(2,1)} async-done(((bf16[32,128,1024]{2,1,0:T(8,128)(2,1)}), bf16[32,128,1024]{2,1,0:T(8,128)(2,1)}, u32[]{:S(2)}, u32[]{:S(2)}) %all-to-all-start) | async-done | bytes 8388640 | tf_op jit(solution)/shard_map/all_to_all | solution.py:52
  133.2 5.1 %multiply_reduce_fusion = f32[32,128]{1,0:T(8,128)S(1)} fusion(bf16[32,128,1024]{2,1,0:T(8,128)(2,1)} %all-to-all-done), kind=kLoop, calls=%fused_computation.2 | loop fusion | flops 12578816 | bytes 8404992 | tf_op jit(solution)/shard_map/reduce_sum | solution.py:14
  138.3 0.1 rsqrt.34
  138.4 4.8 %fusion.7 = f32[32,2,64,128]{3,2,0,1:T(8,128)S(1)} fusion(bf16[32,2,64,1024]{3,2,1,0:T(8,128)(2,1)} %bitcast.16, f32[2,128]{1,0:T(2,128)S(1)} %add_rsqrt_fusion.3, f32[32,2,64]{2,0,1:T(8,128)S(1)} %copy.7, bf16[2,128,1024]{2,1,0:T(8,128)(2,1)S(1)} %copy-done.3), kind=kOutput, calls=%fused_computation.16 | convolution fusion | flops 1075314688 | bytes 11027456 | tf_op jit(solution)/shard_map/sgcd,gkd->sgck/dot_general | solution.py:55
  143.2 1.5 copy.8
  144.7 18.4 %all-to-all-start.1 = ((f32[32,128,128]{2,1,0:T(8,128)}), f32[32,128,128]{2,1,0:T(8,128)S(1)}, u32[]{:S(2)}, u32[]{:S(2)}) async-start(f32[32,128,128]{2,1,0:T(8,128)} %bitcast.53), calls=%async_computation.1 | async-start | bytes 4194304 | tf_op jit(solution)/shard_map/all_to_all | solution.py:58
  163.1 4.3 fusion.14
  167.4 78.3 %psum.42 = f32[1024]{0:T(1024)S(1)} all-reduce(f32[1024]{0:T(1024)S(1)} %bitcast.55), channel_id=1, replica_groups=mesh['cent'=8,'dp'=32] {'dp'}, use_global_device_ids=true, to_apply=%region_2.0 | all-reduce | flops 1024 | bytes 8192 | tf_op jit(solution)/shard_map/psum | solution.py:37
  245.7 5.8 %fusion.17 = f32[1,1024]{1,0:T(1,128)S(1)} fusion(f32[1024,1024]{1,0:T(8,128)} %multiply_exponential_fusion, f32[1024,1]{0,1:T(1,128)S(1)} %bitcast.62), kind=kOutput, calls=%fused_computation.39 | convolution fusion | flops 12582912 | bytes 4202496 | tf_op jit(solution)/shard_map/dot_general | solution.py:38
  251.4 20.2 %psum.43 = f32[1024]{0:T(1024)S(1)} all-reduce(f32[1024]{0:T(1024)S(1)} %bitcast.63), channel_id=1, replica_groups=mesh['cent'=8,'dp'=32] {'cent'}, use_global_device_ids=true, to_apply=%region_3.0 | all-reduce | flops 1024 | bytes 8192 | tf_op jit(solution)/shard_map/psum | solution.py:40
  271.7 4.3 fusion.18
  275.9 62.7 %psum.44 = f32[1024]{0:T(1024)S(1)} all-reduce(f32[1024]{0:T(1024)S(1)} %bitcast.65), channel_id=1, replica_groups=mesh['cent'=8,'dp'=32] {'dp'}, use_global_device_ids=true, to_apply=%region_4.0 | all-reduce | flops 1024 | bytes 8192 | tf_op jit(solution)/shard_map/psum | solution.py:37
  338.6 5.8 %fusion.19 = f32[1,1024]{1,0:T(1,128)S(1)} fusion(f32[1024,1024]{1,0:T(8,128)} %multiply_exponential_fusion, f32[1024,1]{0,1:T(1,128)S(1)} %bitcast.66), kind=kOutput, calls=%fused_computation.41 | convolution fusion | flops 12582912 | bytes 4202496 | tf_op jit(solution)/shard_map/dot_general | solution.py:38
  344.4 0.0 all-to-all-done.1
  344.4 2.8 gather_fusion
  347.2 0.2 reduce_sum.59
  347.4 14.4 %all-reduce = (f32[1024]{0:T(1024)S(1)}, f32[1024]{0:T(1024)S(1)}) all-reduce(f32[1024]{0:T(1024)S(1)} %bitcast.61, f32[1024]{0:T(1024)S(1)} %reduce_sum.59), channel_id=1, replica_groups=mesh['cent'=8,'dp'=32] {'cent'}, use_global_device_ids=true, to_apply=%region_5.0 | all-reduce | flops 2048 | bytes 16384 | tf_op jit(solution)/shard_map/psum | solution.py:40
  361.9 4.3 fusion.20
  366.1 62.7 %psum.46 = f32[1024]{0:T(1024)S(1)} all-reduce(f32[1024]{0:T(1024)S(1)} %bitcast.68), channel_id=1, replica_groups=mesh['cent'=8,'dp'=32] {'dp'}, use_global_device_ids=true, to_apply=%region_6.0 | all-reduce | flops 1024 | bytes 8192 | tf_op jit(solution)/shard_map/psum | solution.py:37
  428.8 0.0 copy-start
  428.8 5.9 %fusion.21 = f32[1,1024]{1,0:T(1,128)S(1)} fusion(f32[1024,1024]{1,0:T(8,128)} %multiply_exponential_fusion, f32[1024,1]{0,1:T(1,128)S(1)} %bitcast.54), kind=kOutput, calls=%fused_computation.43 | convolution fusion | flops 12582912 | bytes 4202496 | tf_op jit(solution)/shard_map/dot_general | solution.py:38
  434.7 2.1 collective-permute-start
  436.8 1.6 collective-permute-done
  438.3 0.2 collective-permute-start.1
  438.6 4.3 collective-permute-done.1
  442.9 3.3 collective-permute-start.2
  446.2 0.9 divide_convert_fusion
  447.1 3.3 collective-permute-done.2
  450.4 0.0 copy-done
  450.4 1.9 multiply_convert_fusion
  (15 shorter events, 0.1 us)
Async XLA Ops:
  13.5 6.2 %copy-start.3 = (bf16[2,128,1024]{2,1,0:T(8,128)(2,1)S(1)}, bf16[2,128,1024]{2,1,0:T(8,128)(2,1)}, u32[]{:S(2)}) copy-start(bf16[2,128,1024]{2,1,0:T(8,128)(2,1)} %param.7) | copy-start | bytes 1572868
  13.5 8.6 %copy-start.1 = (bf16[1024,1024]{1,0:T(8,128)(2,1)S(1)}, bf16[1024,1024]{1,0:T(8,128)(2,1)}, u32[]{:S(2)}) copy-start(bf16[1024,1024]{1,0:T(8,128)(2,1)} %param.4) | copy-start | bytes 6291460
  13.5 119.7 %all-to-all-start = ((bf16[32,128,1024]{2,1,0:T(8,128)(2,1)}), bf16[32,128,1024]{2,1,0:T(8,128)(2,1)}, u32[]{:S(2)}, u32[]{:S(2)}) async-start(bf16[32,128,1024]{2,1,0:T(8,128)(2,1)} %bitcast.51), calls=%async_computation | async-start | bytes 16777216 | tf_op jit(solution)/shard_map/all_to_all | solution.py:52
  19.7 2.9 copy-start.2
  144.7 199.7 %all-to-all-start.1 = ((f32[32,128,128]{2,1,0:T(8,128)}), f32[32,128,128]{2,1,0:T(8,128)S(1)}, u32[]{:S(2)}, u32[]{:S(2)}) async-start(f32[32,128,128]{2,1,0:T(8,128)} %bitcast.53), calls=%async_computation.1 | async-start | bytes 4194304 | tf_op jit(solution)/shard_map/all_to_all | solution.py:58
  428.8 21.6 %copy-start = (f32[1024,1024]{1,0:T(8,128)S(1)}, f32[1024,1024]{1,0:T(8,128)}, u32[]{:S(2)}) copy-start(f32[1024,1024]{1,0:T(8,128)} %multiply_exponential_fusion) | copy-start | bytes 12582916
  434.7 3.6 collective-permute-start
  438.3 4.5 collective-permute-start.1
  442.9 7.5 %collective-permute-start.2 = (f32[1024]{0:T(1024)S(1)}, f32[1024]{0:T(1024)S(1)}, u32[]{:S(2)}, u32[]{:S(2)}) collective-permute-start(f32[1024]{0:T(1024)S(1)} %add.68), channel_id=1, source_target_pairs={{0,128},{32,160},{64,192},{96,224},{128,0},{160,32},{192,64},{224,... | collective-permute-start | bytes 12296 | tf_op jit(solution)/shard_map/ppermute | solution.py:65
